TPU v7x, 256 devices: a whole 4x4x8 slice. The times are simulated.
256 devices in a mesh: dp: 16 (over x, z_lo, core), space: 16 (over y, z_hi).
Axes of the slice: x: 4, y: 4, z: 8 (z_hi: 4, z_lo: 2; z = z_hi * 2 + z_lo), core: 2. Of those that a mesh axis runs over, the one named last changes fastest.
Arguments:
- acts_in: bfloat16 [16, 64, 64, 32, 128], P('dp', 'space'), may hold values from -6 to 6
- pre_act: bfloat16 [16, 64, 64, 32, 128], P('dp', 'space'), may hold values from -6 to 6
- weight_two: bfloat16 [128, 3, 3, 3, 128], P('space'), may hold values from -0.109375 to 0.109375
- grad_out: bfloat16 [16, 32, 32, 16, 128], P('dp', None, None, None, 'space'), may hold values from -6 to 6
Outputs:
- fine_grad: float32 [128, 3, 3, 3, 128], P('space')
- coarse_grad: float32 [128, 3, 3, 3, 128], P('space')
All inputs are finite; a program needn't handle non-finite values.
Results may differ from a plain program's by a relative error of at most 0.003.
Values may be sent and summed in bfloat16 or wider, within the bound.
No kernel may reach another device: no remote copies, remote signals or barrier semaphores. Data moves between devices by JAX's collectives and lax.ppermute only.
A program may use at most 128 MiB of HBM per device.

v0:
```python
import math
import jax
import jax.numpy as jnp
from jax import lax
from jax.sharding import PartitionSpec as P

leak_slope = 0.3
parity_taps = {0: ((1, 0),), 1: ((0, 1), (2, 0))}


def passed_along(block, axis, distance):
    devices = range(lax.axis_size(axis))
    route = [(i - distance, i) for i in devices if i - distance in devices]
    return lax.ppermute(block, axis, route)


def padded_2(shard, sides, width):
    for axis, dim in sides:
        size, length = (lax.axis_size(axis), shard.shape[dim])
        up = [(i, (i + 1) % size) for i in range(size - 1)]
        down = [(j, i) for i, j in up]
        last = lax.slice_in_dim(shard, length - width, length, axis=dim)
        initial = lax.slice_in_dim(shard, 0, width, axis=dim)
        before = lax.ppermute(last, axis, up)
        after = lax.ppermute(initial, axis, down)
        shard = jnp.concatenate([before, shard, after], axis=dim)
    return shard


def transpose_conv(padded, weight):
    rows_x = padded.shape[0] - 1
    rows_y = padded.shape[1] - 1
    rows_z = padded.shape[2] - 1
    outputs = weight.shape[4]
    zpair = jnp.concatenate([padded[:, :, :rows_z, :], padded[:, :, 1:, :]], axis=3)
    nothing = jnp.zeros((weight.shape[0], outputs), weight.dtype)
    classes = []
    for parity_x in (0, 1):
        for parity_y in (0, 1):
            pieces = []
            blocks = []
            for tap_x, move_x in parity_taps[parity_x]:
                for tap_y, move_y in parity_taps[parity_y]:
                    pieces.append(zpair[move_x : move_x + rows_x, move_y : move_y + rows_y])
                    taps = weight[:, tap_x, tap_y]
                    first = jnp.concatenate([taps[:, 1], taps[:, 2]], axis=1)
                    second = jnp.concatenate([nothing, taps[:, 0]], axis=1)
                    blocks.append(jnp.concatenate([first, second], axis=0))
            stacked = jnp.concatenate(pieces, axis=3)
            flat = stacked.reshape(-1, stacked.shape[3])
            mixing = jnp.concatenate(blocks, axis=0)
            classes.append(jnp.dot(flat, mixing, preferred_element_type=jnp.float32))
    joined = jnp.stack(classes).reshape(2, 2, rows_x, rows_y, rows_z, 2 * outputs)
    joined = joined.transpose(2, 0, 3, 1, 4, 5)
    return joined.reshape(2 * rows_x, 2 * rows_y, 2 * rows_z, outputs)


def depth_taps(volume):
    count_x, count_y, count_z, channels = volume.shape
    paired = volume.reshape(count_x, count_y, count_z // 2, 2 * channels)
    even = paired[..., :channels]
    odd = paired[..., channels:]
    earlier = jnp.pad(odd[:, :, :-1, :], ((0, 0), (0, 0), (1, 0), (0, 0)))
    return jnp.concatenate([earlier, even, odd], axis=3)


def coarse_terms(hidden, below, gradient):
    count_x, count_y, count_z, filters = gradient.shape
    flat_grad = gradient.reshape(-1, filters)
    stacked = depth_taps(hidden)
    width = stacked.shape[3]
    split = stacked.reshape(count_x, 2, count_y, 2, count_z, width)
    rim = depth_taps(below).reshape(1, count_y, 2, count_z, width)
    by_x = [jnp.concatenate([rim, split[:-1, 1]], axis=0), split[:, 0], split[:, 1]]
    terms = []
    for tap_x in range(3):
        plane = by_x[tap_x]
        by_y = [
            jnp.pad(plane[:, :-1, 1], ((0, 0), (1, 0), (0, 0), (0, 0))),
            plane[:, :, 0],
            plane[:, :, 1],
        ]
        for tap_y in range(3):
            piece = by_y[tap_y].reshape(-1, width)
            terms.append(
                lax.dot_general(
                    flat_grad, piece, (((0,), (0,)), ((), ())), preferred_element_type=jnp.float32
                )
            )
    return jnp.stack(terms, axis=1).reshape(filters, 3, 3, 3, width // 3)


def fine_terms(framed, gradient):
    count_x, count_y, count_z, filters = gradient.shape
    flat_grad = gradient.reshape(-1, filters)
    stacked = jnp.concatenate(
        [framed[:, :, shift : shift + count_z, :] for shift in range(3)], axis=3
    )
    width = stacked.shape[3]
    terms = []
    for tap_x in range(3):
        for tap_y in range(3):
            piece = stacked[tap_x : tap_x + count_x, tap_y : tap_y + count_y].reshape(-1, width)
            terms.append(
                lax.dot_general(
                    flat_grad, piece, (((0,), (0,)), ((), ())), preferred_element_type=jnp.float32
                )
            )
    return jnp.stack(terms, axis=1).reshape(filters, 3, 3, 3, width // 3)


def filter_share(whole_terms):
    return lax.psum_scatter(whole_terms, "space", scatter_dimension=0, tiled=True)


def body(acts_in, pre_act, weight_two, grad_out):
    parts = lax.axis_size("space")
    groups = lax.axis_size("dp")
    acts = acts_in[0]
    depth, across, height, channels = acts.shape
    scaling = 1.0 / math.sqrt(groups * depth * parts * across * height)
    before_f = pre_act[0].astype(jnp.float32)
    hidden = jnp.where(before_f > 0, before_f, leak_slope * before_f).astype(jnp.bfloat16)
    grad_tile = lax.all_to_all(grad_out, "space", split_axis=1, concat_axis=4, tiled=True)[0]
    below = passed_along(hidden[-1:], "space", 1)
    whole_weight = lax.all_gather(weight_two, "space", axis=0, tiled=True)
    above = passed_along(grad_tile[:1], "space", -1)
    upper = jnp.pad(jnp.concatenate([grad_tile, above], axis=0), ((0, 0), (0, 1), (0, 1), (0, 0)))
    back = transpose_conv(upper, whole_weight)
    delta = (back * jnp.where(before_f > 0, 1.0, leak_slope)).astype(jnp.bfloat16)
    framed = padded_2(acts, (("space", 0),), 1)
    framed = jnp.pad(framed, ((0, 0), (1, 1), (1, 1), (0, 0)))
    coarse_full = coarse_terms(hidden, below, grad_tile)
    fine_full = fine_terms(framed, delta)
    coarse_all, fine_all = lax.psum((coarse_full, fine_full), "dp")
    coarse_sum = filter_share(coarse_all)
    fine_sum = filter_share(fine_all)
    return (fine_sum * scaling, coarse_sum * scaling)


def solution(mesh):
    placed = (
        P("dp", "space", None, None, None),
        P("dp", "space", None, None, None),
        P("space", None, None, None, None),
        P("dp", None, None, None, "space"),
    )
    return jax.shard_map(
        body,
        mesh=mesh,
        in_specs=placed,
        out_specs=(P("space", None, None, None, None), P("space", None, None, None, None)),
        check_vma=False,
    )
```

profile of v0, /device:TPU:1, one launch (start us, length us, event | category | flops | bytes accessed | tf_op | source)
XLA Modules:
  0.0 557.8 jit_solution(2859011999417366187)
XLA Ops:
  10.2 11.7 %all-to-all-start = ((bf16[16,2,4096]{2,1,0:T(2,128)(2,1)}), bf16[16,2,4096]{2,1,0:T(2,128)(2,1)S(1)}, u32[]{:S(2)}, u32[]{:S(2)}) async-start(bf16[16,2,4096]{2,1,0:T(2,128)(2,1)} %reshape.94), calls=%async_computation | async-start | bytes 524288 | tf_op jit(solution)/shard_map/all_to_all | solution.py:124
  22.0 2.3 slice_bitcast_fusion.7
  24.3 5.0 collective-permute-start.1
  30.5 2.7 reshape.82
  33.2 2.8 fusion.22
  40.5 51.2 %all_gather.3 = bf16[128,3,3,3,128]{4,0,3,2,1:T(8,128)(2,1)S(1)} all-gather(bf16[8,3,3,3,128]{4,0,3,2,1:T(8,128)(2,1)S(1)} %copy-done.13), channel_id=1, replica_groups=mesh['dp'=16,'space'=16] {'space'}, dimensions={0}, use_global_device_ids=true | all-gather | bytes 940032 | tf_op jit(solution)/shard_map/all_gather | solution.py:126
  100.8 2.6 convert_bitcast_fusion
  105.1 3.6 reshape_squeeze.21
  111.8 2.8 copy.55
  114.5 4.6 select_maximum_fusion
  119.1 3.8 fusion.164
  122.9 8.0 %pad_maximum_fusion = bf16[6,66,32,384]{3,2,1,0:T(8,128)(2,1)} fusion(bf16[6,66,32,128]{3,2,1,0:T(8,128)(2,1)} %get-tuple-element.16, bf16[6,66,32,128]{3,2,1,0:T(8,128)(2,1)} %get-tuple-element.15, bf16[6,66,32,128]{3,2,1,0:T(8,128)(2,1)S(1)} %get-tuple-element.14), kind=kLoop, calls=%fused_computation.5 | loop fusion | flops 29196288 | bytes 19464192 | tf_op jit(solution)/shard_map/concatenate | solution.py:96
  139.6 2.6 copy.57
  142.2 4.9 reshape.73
  147.1 3.4 multiply_convert_fusion
  151.9 4.7 collective-permute-start.3
  156.7 4.9 fusion.45
  163.6 2.0 fusion.57
  165.6 2.0 fusion.63
  177.4 2.3 copy.58
  179.6 2.5 copy.59
  187.7 2.5 copy.60
  192.2 234.4 %all-reduce.23.cloned.1.call-done = (f32[128,3,3,3,128]{4,3,2,1,0:T(4,128)}, f32[128,3,3,3,128]{4,3,2,1,0:T(4,128)}) async-done(((f32[128,3,3,3,128]{4,3,2,1,0:T(4,128)}, f32[128,3,3,3,128]{4,3,2,1,0:T(4,128)}), (f32[128,3,3,3,128]{4,3,2,1,0:T(4,128)}, f32[128,3,3,3,128]{4,3,2,1,0:T(4,128)})) %all-reduce.23.cloned.1.call-update) | async-done | bytes 3538960
  429.9 117.9 %all-reduce.25.cloned.1.call-done = (f32[8,3,3,3,128]{4,3,2,1,0:T(4,128)}, f32[8,3,3,3,128]{4,3,2,1,0:T(4,128)}) async-done(((f32[8,3,3,3,128]{4,3,2,1,0:T(4,128)}, f32[8,3,3,3,128]{4,3,2,1,0:T(4,128)}), (f32[8,3,3,3,128]{4,3,2,1,0:T(4,128)}, f32[8,3,3,3,128]{4,3,2,1,0:T(4,128)})) %all-reduce.25.cloned.1.call-update) | async-done | bytes 221200 | tf_op jit(solution)/shard_map/psum | solution.py:135
  (142 shorter events, 57.2 us)
Async XLA Ops:
  8.5 22.0 %copy-start.2 = (bf16[1,4,64,32,128]{4,3,2,1,0:T(8,128)(2,1)S(1)}, bf16[1,4,64,32,128]{4,3,2,1,0:T(8,128)(2,1)}, u32[]{:S(2)}) copy-start(bf16[1,4,64,32,128]{4,3,2,1,0:T(8,128)(2,1)} %param.5) | copy-start | bytes 6291460
  10.2 93.2 %all-to-all-start = ((bf16[16,2,4096]{2,1,0:T(2,128)(2,1)}), bf16[16,2,4096]{2,1,0:T(2,128)(2,1)S(1)}, u32[]{:S(2)}, u32[]{:S(2)}) async-start(bf16[16,2,4096]{2,1,0:T(2,128)(2,1)} %reshape.94), calls=%async_computation | async-start | bytes 524288 | tf_op jit(solution)/shard_map/all_to_all | solution.py:124
  22.0 404.7 %all-reduce.23.cloned.1.call-start = ((), (), s32[]{:S(2)}) async-start(), calls=%async_computation.1 | async-start | bytes 9437184
  24.3 90.2 %collective-permute-start.1 = (bf16[1,64,32,128]{3,2,1,0:T(8,128)(2,1)}, bf16[1,64,32,128]{3,2,1,0:T(8,128)(2,1)}, u32[]{:S(2)}, u32[]{:S(2)}) collective-permute-start(bf16[1,64,32,128]{3,2,1,0:T(8,128)(2,1)} %get-tuple-element.19), channel_id=1, source_target_pairs={{0,1},{1,2},{2,3},{3,4},{4,5},{5,6},{6,7},{7,8},{8,9},{9,10},{10,1... | collective-permute-start | bytes 1572872 | tf_op jit(solution)/shard_map/ppermute | solution.py:24
  29.2 85.3 %collective-permute-start.2 = (bf16[1,64,32,128]{3,2,1,0:T(8,128)(2,1)}, bf16[1,64,32,128]{3,2,1,0:T(8,128)(2,1)}, u32[]{:S(2)}, u32[]{:S(2)}) collective-permute-start(bf16[1,64,32,128]{3,2,1,0:T(8,128)(2,1)} %get-tuple-element.20), channel_id=1, source_target_pairs={{1,0},{2,1},{3,2},{4,3},{5,4},{6,5},{7,6},{8,7},{9,8},{10,9},{11,1... | collective-permute-start | bytes 1572872 | tf_op jit(solution)/shard_map/ppermute | solution.py:25
  38.7 1.8 copy-start.13
  110.3 22.4 %collective-permute-start = (bf16[1,32,16,128]{1,3,2,0:T(8,128)(2,1)}, bf16[1,32,16,128]{1,3,2,0:T(8,128)(2,1)}, u32[]{:S(2)}, u32[]{:S(2)}) collective-permute-start(bf16[1,32,16,128]{1,3,2,0:T(8,128)(2,1)} %bitcast.329), channel_id=1, source_target_pairs={{1,0},{2,1},{3,2},{4,3},{5,4},{6,5},{7,6},{8,7},{9,8},{10,9},{11,1... | collective-permute-start | bytes 393224 | tf_op jit(solution)/shard_map/ppermute | solution.py:14
  135.9 1.9 copy-start.11
  135.9 1.9 copy-start.12
  135.9 2.3 copy-start.14
  135.9 2.3 copy-start.15
  135.9 2.3 copy-start.16
  136.0 2.3 copy-start.17
  136.0 2.3 copy-start.18
  136.0 2.3 copy-start.19
  142.2 4.9 copy-start.3
  147.1 14.5 %slice-start = ((s8[9732096]{0:T(1024)(128)(4,1)}), s8[1343488]{0:T(1024)(128)(4,1)S(1)}, s32[]{:S(2)}) async-start(s8[9732096]{0:T(1024)(128)(4,1)} %bitcast.309), calls=%async_computation.3 | async-start | bytes 2686976
  147.1 14.5 %slice-start.1 = ((s8[9732096]{0:T(1024)(128)(4,1)}), s8[4194304]{0:T(1024)(128)(4,1)S(1)}, s32[]{:S(2)}) async-start(s8[9732096]{0:T(1024)(128)(4,1)} %bitcast.309), calls=%async_computation.4 | async-start | bytes 8388608
  151.9 30.2 %collective-permute-start.3 = (bf16[1,64,32,128]{3,2,1,0:T(8,128)(2,1)S(1)}, bf16[1,64,32,128]{3,2,1,0:T(8,128)(2,1)S(1)}, u32[]{:S(2)}, u32[]{:S(2)}) collective-permute-start(bf16[1,64,32,128]{3,2,1,0:T(8,128)(2,1)S(1)} %fusion.96), channel_id=1, source_target_pairs={{0,1},{1,2},{2,3},{3,4},{4,5},{5,6},{6,7},{7,8},{8,9},{9,10},{10,1... | collective-permute-start | bytes 1572872 | tf_op jit(solution)/shard_map/ppermute | solution.py:14
  156.6 4.9 slice-start.2
  184.2 1.8 copy-start.6
  184.7 1.8 copy-start.8
  190.2 360.7 %copy-start.1 = (bf16[1,32,32,16,8]{2,4,3,1,0:T(8,128)(2,1)S(1)}, bf16[1,32,32,16,8]{2,4,3,1,0:T(8,128)(2,1)}, u32[]{:S(2)}) copy-start(bf16[1,32,32,16,8]{2,4,3,1,0:T(8,128)(2,1)} %param.7) | copy-start | bytes 786436
  190.3 357.5 %all-reduce.25.cloned.1.call-start = ((), (), s32[]{:S(2)}) async-start(), calls=%async_computation.2 | async-start | bytes 589824 | tf_op jit(solution)/shard_map/psum | solution.py:135
  (13 other events, 14.9 us)
Sparse Core Ops, SparseCore 0:
  190.4 236.2 all-reduce.22
  430.0 117.7 all-reduce.24
where the time goes:
time: 559 us; the launch traced here: 558 us
  waiting for transfers between devices  354 us (63%)
  local copies, waits for them, and re-layouts  54.9 us (10%)
  blocking collectives  51.2 us (9%)
  other arithmetic  30.5 us (5%)
  matrix products  27.4 us (5%)
  starting transfers between devices  24.2 us (4%)
  between operations  15.4 us (3%)
    unnamed x3, waiting for transfers between devices  234 us
    psum x1, waiting for transfers between devices, body(): coarse_all, fine_all = lax.psum((coarse_full, fine_full), 'dp')  118 us
    all_gather x1, blocking collectives, body(): whole_weight = lax.all_gather(weight_two, 'space', axis=0, tiled=True)  51.2 us
    dot_general x9, matrix products, fine_terms(): lax.dot_general(flat_grad, piece, (((0,), (0,)), ((), ())), preferred_ele...  20.7 us
    unnamed x71, local copies, waits for them, and re-layouts  11.9 us
    all_to_all x1, starting transfers between devices, body(): lax.all_to_all(grad_out, 'space', split_axis=1, concat_axis=4, tiled=True)  11.7 us
  transfers between devices with their start and end apart: 7, of which 3 were waited for; matrix products, arithmetic and copies ran while one was open for 14% of the time, Pallas kernels for 0%

commit v1 on v0

--- a/solution.py
+++ b/solution.py
@@ -123,7 +123,9 @@
     hidden = jnp.where(before_f > 0, before_f, leak_slope * before_f).astype(jnp.bfloat16)
     grad_tile = lax.all_to_all(grad_out, "space", split_axis=1, concat_axis=4, tiled=True)[0]
     below = passed_along(hidden[-1:], "space", 1)
-    whole_weight = lax.all_gather(weight_two, "space", axis=0, tiled=True)
+    whole_weight = jnp.concatenate(
+        lax.all_to_all(jnp.stack([weight_two] * lax.axis_size("space")), "space", 0, 0), axis=0
+    )
     above = passed_along(grad_tile[:1], "space", -1)
     upper = jnp.pad(jnp.concatenate([grad_tile, above], axis=0), ((0, 0), (0, 1), (0, 1), (0, 0)))
     back = transpose_conv(upper, whole_weight)

time: 559 us -> 531 us (0.950); the launches traced: 558 us -> 523 us
  blocking collectives: 51.2 us -> 0 us
  starting transfers between devices: 24.2 us -> 35.1 us
    all_gather x1 -> x0, blocking collectives: 51.2 us -> none  [body(): whole_weight = lax.all_gather(weight_two, 'space', axis=0, tiled=True)]
    ppermute x2, waiting for transfers between devices: 1.76 us -> 13.6 us  [passed_along(): return lax.ppermute(block, axis, route)]
    all_to_all x0 -> x1, starting transfers between devices: none -> 10.2 us  [body(): lax.all_to_all(jnp.stack([weight_two] * lax.axis_size('space')), 'space',...]
    unnamed x3, waiting for transfers between devices: 234 us -> 226 us
    unnamed x71 -> x47, local copies, waits for them, and re-layouts: 11.9 us -> 13.4 us
  transfers between devices with their start and end apart: 7 -> 8, of which waited for: 3 -> 3; matrix products, arithmetic and copies ran while one was open for 14% -> 15% of each run, Pallas kernels for 0% -> 0%
where the time goes in v1:
time: 531 us; the launch traced here: 523 us
  waiting for transfers between devices  357 us (67%)
  local copies, waits for them, and re-layouts  58.6 us (11%)
  starting transfers between devices  35.1 us (7%)
  other arithmetic  30.2 us (6%)
  matrix products  26.3 us (5%)
  between operations  15.6 us (3%)
    unnamed x3, waiting for transfers between devices  226 us
    psum x1, waiting for transfers between devices, body(): coarse_all, fine_all = lax.psum((coarse_full, fine_full), 'dp')  118 us
    dot_general x9, matrix products, fine_terms(): lax.dot_general(flat_grad, piece, (((0,), (0,)), ((), ())), preferred_ele...  20.7 us
    ppermute x2, waiting for transfers between devices, passed_along(): return lax.ppermute(block, axis, route)  13.6 us
    unnamed x47, local copies, waits for them, and re-layouts  13.4 us
    all_to_all x1, starting transfers between devices, body(): lax.all_to_all(grad_out, 'space', split_axis=1, concat_axis=4, tiled=True)  11.7 us
  transfers between devices with their start and end apart: 8, of which 3 were waited for; matrix products, arithmetic and copies ran while one was open for 15% of the time, Pallas kernels for 0%

profile of v1, /device:TPU:1, one launch (start us, length us, event | category | flops | bytes accessed | tf_op | source)
XLA Modules:
  0.0 523.1 jit_solution(3914645068038190603)
XLA Ops:
  9.5 3.2 reshape.100
  12.7 11.7 %all-to-all-start = ((bf16[16,2,4096]{2,1,0:T(2,128)(2,1)}), bf16[16,2,4096]{2,1,0:T(2,128)(2,1)S(1)}, u32[]{:S(2)}, u32[]{:S(2)}) async-start(bf16[16,2,4096]{2,1,0:T(2,128)(2,1)} %reshape.100), calls=%async_computation | async-start | bytes 524288 | tf_op jit(solution)/shard_map/all_to_all | solution.py:124
  24.5 2.3 slice_bitcast_fusion.7
  26.7 5.0 collective-permute-start.1
  33.0 2.6 reshape.88
  35.6 2.8 fusion.22
  44.7 2.6 convert_bitcast_fusion
  48.5 10.2 %all-to-all-start.1 = ((bf16[16,8,3,3,3,128]{5,1,4,3,2,0:T(8,128)(2,1)}), bf16[16,8,3,3,3,128]{5,1,4,3,2,0:T(8,128)(2,1)}, u32[]{:S(2)}, u32[]{:S(2)}) async-start(bf16[16,8,3,3,3,128]{5,1,4,3,2,0:T(8,128)(2,1)} %stack.94), calls=%async_computation.1 | async-start | bytes 1769472 | tf_op jit(solution)/shard_map/all_to_all | solution.py:127
  61.5 3.6 reshape_squeeze.21
  71.1 4.6 select_maximum_fusion
  75.7 5.2 fusion.164
  80.9 9.0 %pad_maximum_fusion = bf16[6,66,32,384]{3,2,1,0:T(8,128)(2,1)} fusion(bf16[6,66,32,128]{3,2,1,0:T(8,128)(2,1)} %get-tuple-element.16, bf16[6,66,32,128]{3,2,1,0:T(8,128)(2,1)} %get-tuple-element.15, bf16[6,66,32,128]{3,2,1,0:T(8,128)(2,1)} %get-tuple-element.14), kind=kLoop, calls=%fused_computation.5 | loop fusion | flops 29196288 | bytes 19464192 | tf_op jit(solution)/shard_map/concatenate | solution.py:96
  89.8 13.6 %collective-permute-done = bf16[1,32,16,128]{1,3,2,0:T(8,128)(2,1)} collective-permute-done((bf16[1,32,16,128]{1,3,2,0:T(8,128)(2,1)S(1)}, bf16[1,32,16,128]{1,3,2,0:T(8,128)(2,1)}, u32[]{:S(2)}, u32[]{:S(2)}) %collective-permute-start) | collective-permute-done | bytes 131104 | tf_op jit(solution)/shard_map/ppermute | solution.py:14
  111.9 2.6 copy.72
  114.5 4.9 reshape.79
  119.4 3.4 multiply_convert_fusion
  122.8 2.2 fusion.96
  125.1 5.0 collective-permute-start.3
  130.1 4.9 fusion.45
  150.8 2.5 copy.73
  153.3 2.5 copy.74
  161.3 2.5 copy.75
  165.9 225.8 %all-reduce.23.cloned.1.call-done = (f32[128,3,3,3,128]{4,3,2,1,0:T(4,128)}, f32[128,3,3,3,128]{4,3,2,1,0:T(4,128)}) async-done(((f32[128,3,3,3,128]{4,3,2,1,0:T(4,128)}, f32[128,3,3,3,128]{4,3,2,1,0:T(4,128)}), (f32[128,3,3,3,128]{4,3,2,1,0:T(4,128)}, f32[128,3,3,3,128]{4,3,2,1,0:T(4,128)})) %all-reduce.23.cloned.1.call-update) | async-done | bytes 3538960
  394.9 117.9 %all-reduce.25.cloned.1.call-done = (f32[8,3,3,3,128]{4,3,2,1,0:T(4,128)}, f32[8,3,3,3,128]{4,3,2,1,0:T(4,128)}) async-done(((f32[8,3,3,3,128]{4,3,2,1,0:T(4,128)}, f32[8,3,3,3,128]{4,3,2,1,0:T(4,128)}), (f32[8,3,3,3,128]{4,3,2,1,0:T(4,128)}, f32[8,3,3,3,128]{4,3,2,1,0:T(4,128)})) %all-reduce.25.cloned.1.call-update) | async-done | bytes 221200 | tf_op jit(solution)/shard_map/psum | solution.py:137
  (121 shorter events, 56.8 us)
Async XLA Ops:
  7.2 1.2 copy-start
  9.5 23.5 %copy-start.2 = (bf16[1,4,64,32,128]{4,3,2,1,0:T(8,128)(2,1)S(1)}, bf16[1,4,64,32,128]{4,3,2,1,0:T(8,128)(2,1)}, u32[]{:S(2)}) copy-start(bf16[1,4,64,32,128]{4,3,2,1,0:T(8,128)(2,1)} %param.5) | copy-start | bytes 6291460
  12.7 34.7 %all-to-all-start = ((bf16[16,2,4096]{2,1,0:T(2,128)(2,1)}), bf16[16,2,4096]{2,1,0:T(2,128)(2,1)S(1)}, u32[]{:S(2)}, u32[]{:S(2)}) async-start(bf16[16,2,4096]{2,1,0:T(2,128)(2,1)} %reshape.100), calls=%async_computation | async-start | bytes 524288 | tf_op jit(solution)/shard_map/all_to_all | solution.py:124
  26.7 44.3 %collective-permute-start.1 = (bf16[1,64,32,128]{3,2,1,0:T(8,128)(2,1)}, bf16[1,64,32,128]{3,2,1,0:T(8,128)(2,1)}, u32[]{:S(2)}, u32[]{:S(2)}) collective-permute-start(bf16[1,64,32,128]{3,2,1,0:T(8,128)(2,1)} %get-tuple-element.19), channel_id=1, source_target_pairs={{0,1},{1,2},{2,3},{3,4},{4,5},{5,6},{6,7},{7,8},{8,9},{9,10},{10,1... | collective-permute-start | bytes 1572872 | tf_op jit(solution)/shard_map/ppermute | solution.py:24
  31.7 39.4 %collective-permute-start.2 = (bf16[1,64,32,128]{3,2,1,0:T(8,128)(2,1)}, bf16[1,64,32,128]{3,2,1,0:T(8,128)(2,1)}, u32[]{:S(2)}, u32[]{:S(2)}) collective-permute-start(bf16[1,64,32,128]{3,2,1,0:T(8,128)(2,1)} %get-tuple-element.20), channel_id=1, source_target_pairs={{1,0},{2,1},{3,2},{4,3},{5,4},{6,5},{7,6},{8,7},{9,8},{10,9},{11,1... | collective-permute-start | bytes 1572872 | tf_op jit(solution)/shard_map/ppermute | solution.py:25
  44.7 2.7 copy-start.13
  48.5 58.5 %all-to-all-start.1 = ((bf16[16,8,3,3,3,128]{5,1,4,3,2,0:T(8,128)(2,1)}), bf16[16,8,3,3,3,128]{5,1,4,3,2,0:T(8,128)(2,1)}, u32[]{:S(2)}, u32[]{:S(2)}) async-start(bf16[16,8,3,3,3,128]{5,1,4,3,2,0:T(8,128)(2,1)} %stack.94), calls=%async_computation.1 | async-start | bytes 1769472 | tf_op jit(solution)/shard_map/all_to_all | solution.py:127
  58.7 332.9 %all-reduce.23.cloned.1.call-start = ((), (), s32[]{:S(2)}) async-start(), calls=%async_computation.2 | async-start | bytes 9437184
  67.2 36.3 %collective-permute-start = (bf16[1,32,16,128]{1,3,2,0:T(8,128)(2,1)S(1)}, bf16[1,32,16,128]{1,3,2,0:T(8,128)(2,1)}, u32[]{:S(2)}, u32[]{:S(2)}) collective-permute-start(bf16[1,32,16,128]{1,3,2,0:T(8,128)(2,1)S(1)} %bitcast.333), channel_id=1, source_target_pairs={{1,0},{2,1},{3,2},{4,3},{5,4},{6,5},{7,6},{8,7},{9,8},{10,9},{11,1... | collective-permute-start | bytes 393224 | tf_op jit(solution)/shard_map/ppermute | solution.py:14
  109.4 1.2 copy-start.12
  109.5 1.6 copy-start.11
  114.5 4.9 copy-start.3
  119.4 15.7 %slice-start = ((s8[9732096]{0:T(1024)(128)(4,1)}), s8[1343488]{0:T(1024)(128)(4,1)S(1)}, s32[]{:S(2)}) async-start(s8[9732096]{0:T(1024)(128)(4,1)} %bitcast.312), calls=%async_computation.4 | async-start | bytes 2686976
  119.4 15.7 %slice-start.1 = ((s8[9732096]{0:T(1024)(128)(4,1)}), s8[4194304]{0:T(1024)(128)(4,1)S(1)}, s32[]{:S(2)}) async-start(s8[9732096]{0:T(1024)(128)(4,1)} %bitcast.312), calls=%async_computation.5 | async-start | bytes 8388608
  125.1 30.7 %collective-permute-start.3 = (bf16[1,64,32,128]{3,2,1,0:T(8,128)(2,1)}, bf16[1,64,32,128]{3,2,1,0:T(8,128)(2,1)S(1)}, u32[]{:S(2)}, u32[]{:S(2)}) collective-permute-start(bf16[1,64,32,128]{3,2,1,0:T(8,128)(2,1)} %fusion.96), channel_id=1, source_target_pairs={{0,1},{1,2},{2,3},{3,4},{4,5},{5,6},{6,7},{7,8},{8,9},{9,10},{10,1... | collective-permute-start | bytes 1572872 | tf_op jit(solution)/shard_map/ppermute | solution.py:14
  130.1 5.0 slice-start.2
  157.3 1.4 copy-start.9
  157.4 1.8 copy-start.7
  157.8 1.8 copy-start.6
  158.3 1.8 copy-start.8
  158.7 1.7 copy-start.5
  159.2 1.7 copy-start.4
  163.8 352.2 %copy-start.1 = (bf16[1,32,32,16,8]{2,4,3,1,0:T(8,128)(2,1)S(1)}, bf16[1,32,32,16,8]{2,4,3,1,0:T(8,128)(2,1)}, u32[]{:S(2)}) copy-start(bf16[1,32,32,16,8]{2,4,3,1,0:T(8,128)(2,1)} %param.7) | copy-start | bytes 786436
  163.9 348.9 %all-reduce.25.cloned.1.call-start = ((), (), s32[]{:S(2)}) async-start(), calls=%async_computation.3 | async-start | bytes 589824 | tf_op jit(solution)/shard_map/psum | solution.py:137
  (2 other events, 1.9 us)
Sparse Core Ops, SparseCore 0:
  164.0 227.6 all-reduce.22
  395.0 117.7 all-reduce.24
